TPU v7x, 32 devices: a whole 2x2x4 slice. The times are simulated.
32 devices in a mesh: rows: 4 (over x, core), aux: 8 (over z, y).
Axes of the slice: x: 2, y: 2, z: 4, core: 2. Of those that a mesh axis runs over, the one named last changes fastest.
Arguments:
- b_rows: bfloat16 [6144, 8192], P(('rows', 'aux')), may hold values from -0.079589844 to 0.079589844
- pair_index: int32 [6144], P(('rows', 'aux')), may hold values from 0 to 6143, each once
- e_occ: float32 [512], replicated, may hold values from -3 to -0.5
- e_vir: float32 [1536], replicated, may hold values from 0.2 to 3
- occ_batch: int32 [1], replicated, may hold values from 0 to 127
- freq: float32 [1], replicated, may hold values from 0.3 to 3
Outputs:
- q_matrix: float32 [8192, 8192], P('aux', 'rows')
All inputs are finite; a program needn't handle non-finite values.
Results may differ from a plain program's by a relative error of at most 0.0022.
Values may be sent and summed in bfloat16 or wider, within the bound.
No kernel may reach another device: no remote copies, remote signals or barrier semaphores. Data moves between devices by JAX's collectives and lax.ppermute only.
A program may use at most 192 MiB of HBM per device.

v0:
```python
import jax
import jax.numpy as jnp
from jax import lax
from jax.sharding import PartitionSpec as P

NVIR = 1536
NOCC_B = 4


def row_weights(pairs, e_occ, e_vir, occ_batch, freq):
    batch_start = occ_batch[0] * NOCC_B
    e_batch = lax.dynamic_slice_in_dim(e_occ, batch_start, NOCC_B, 0)
    occ = pairs // NVIR
    vir = pairs % NVIR
    occ_hit = occ[:, None] == jnp.arange(NOCC_B, dtype=jnp.int32)[None, :]
    vir_hit = vir[:, None] == jnp.arange(e_vir.shape[0], dtype=jnp.int32)[None, :]
    e_low = jnp.sum(jnp.where(occ_hit, e_batch[None, :], 0.0), axis=1)
    e_high = jnp.sum(jnp.where(vir_hit, e_vir[None, :], 0.0), axis=1)
    delta = e_high - e_low
    return 2.0 * delta / (delta * delta + freq[0] * freq[0])


def contract(left, right):
    return lax.dot_general(
        left, right, (((0,), (0,)), ((), ())), preferred_element_type=jnp.float32
    )


def body(b_rows, pair_index, e_occ, e_vir, occ_batch, freq):
    group_pairs = lax.all_gather(pair_index, "aux", axis=0, tiled=True)
    regrouped = lax.all_to_all(b_rows, "aux", split_axis=1, concat_axis=0, tiled=True)
    weight = row_weights(group_pairs, e_occ, e_vir, occ_batch, freq)
    scaled = (weight[:, None] * regrouped.astype(jnp.float32)).astype(jnp.bfloat16)
    partial_value = contract(scaled, lax.all_gather(regrouped, "aux", axis=1, tiled=True))
    return lax.psum_scatter(partial_value, "rows", scatter_dimension=1, tiled=True)


def solution(mesh):
    placed = (P(("rows", "aux"), None), P(("rows", "aux")), P(), P(), P(), P())
    return jax.shard_map(
        body, mesh=mesh, in_specs=placed, out_specs=P("aux", "rows"), check_vma=False
    )
```

profile of v0, /device:TPU:0, one launch (start us, length us, event | category | flops | bytes accessed | tf_op | source)
XLA Modules:
  0.0 842.8 jit_solution(14496598981891353015)
XLA Ops:
  6.5 0.0 copy-start.2
  6.5 0.0 copy-start
  6.5 0.0 copy-start.1
  6.5 0.0 all-gather.2.cloned.1.call-start
  6.5 2.4 copy.12
  8.9 77.9 %all_to_all.19 = bf16[192,8,1024]{2,0,1:T(8,128)(2,1)} all-to-all(bf16[192,8,1024]{2,0,1:T(8,128)(2,1)S(1)} %bitcast.13), channel_id=1, replica_groups=mesh['rows'=4,'aux'=8] {'aux'}, dimensions={1} | all-to-all | bytes 6291456 | tf_op jit(solution)/shard_map/all_to_all | solution.py:31
  86.8 0.0 all-gather.2.cloned.1.call-update
  86.8 0.0 reduce-scatter.2.cloned.1.call-start
  88.2 0.0 copy-done.2
  88.2 0.6 dynamic-slice
  89.4 0.8 dynamic_slice.3
  90.2 0.0 copy-done
  90.2 0.2 dynamic-update-slice
  90.4 42.0 %all-reduce = s32[1536]{0:T(1024)S(1)} all-reduce(s32[1536]{0:T(1024)S(1)} %dynamic-update-slice), channel_id=1, replica_groups=mesh['rows'=4,'aux'=8] {'aux'}, use_global_device_ids=true, to_apply=%add | all-reduce | flops 1536 | bytes 12288
  132.4 0.1 select_reduce_fusion.1
  132.5 0.0 copy-done.1
  132.5 1.3 select_reduce_fusion
  133.8 432.7 %all-gather.2.cloned.1.call-done = bf16[1536,8192]{1,0:T(8,128)(2,1)} async-done(((bf16[1536,1024]{1,0:T(8,128)(2,1)}), bf16[1536,8192]{1,0:T(8,128)(2,1)}) %all-gather.2.cloned.1.call-update) | async-done | bytes 25165840 | tf_op jit(solution)/shard_map/all_gather | solution.py:34
  566.5 34.5 %fusion = f32[1024,8192]{1,0:T(8,128)} fusion(bf16[1536,8192]{1,0:T(8,128)(2,1)} %all-gather.2.cloned.1.call-done, bf16[1536,1024]{1,0:T(8,128)(2,1)} %bitcast.12, f32[1536]{0:T(1024)S(1)} %add_divide_fusion), kind=kOutput, calls=%fused_computation.3 | convolution fusion | flops 25774522368 | bytes 61872128 | tf_op jit(solution)/shard_map/dot_general | solution.py:24
  601.0 0.0 reduce-scatter.2.cloned.1.call-update
  601.0 234.9 %reduce-scatter.2.cloned.1.call-done = f32[1024,2048]{1,0:T(8,128)} async-done(((f32[1024,8192]{1,0:T(8,128)}), f32[1024,2048]{1,0:T(8,128)}) %reduce-scatter.2.cloned.1.call-update) | async-done | bytes 8388624 | tf_op jit(solution)/shard_map/reduce_scatter | solution.py:35
  (3 shorter events, 0.0 us)
Async XLA Ops:
  6.5 81.6 %copy-start.2 = (u32[32]{0:T(128)S(1)}, u32[32]{0:T(128)}, u32[]{:S(2)}) copy-start(u32[32]{0:T(128)} %constant.32) | copy-start | bytes 388
  6.5 83.7 %copy-start = (s32[192]{0:T(256)S(1)}, s32[192]{0:T(256)}, u32[]{:S(2)}) copy-start(s32[192]{0:T(256)} %param.7) | copy-start | bytes 2308
  6.5 126.0 %copy-start.1 = (f32[1536]{0:T(1024)S(1)}, f32[1536]{0:T(1024)}, u32[]{:S(2)}) copy-start(f32[1536]{0:T(1024)} %param.9) | copy-start | bytes 18436
  6.5 560.0 %all-gather.2.cloned.1.call-start = ((), (), s32[]{:S(2)}) async-start(), calls=%async_computation.2 | async-start | bytes 28311552 | tf_op jit(solution)/shard_map/all_gather | solution.py:34
  86.8 749.1 %reduce-scatter.2.cloned.1.call-start = ((), (), s32[]{:S(2)}) async-start(), calls=%async_computation.3 | async-start | bytes 41943040 | tf_op jit(solution)/shard_map/reduce_scatter | solution.py:35
Sparse Core Ops, SparseCore 0:
  86.9 479.5 all-gather.1
  601.2 234.7 reduce-scatter.1
where the time goes:
time: 843 us
  waiting for transfers between devices  668 us (79%)
  blocking collectives  120 us (14%)
  matrix products  34.5 us (4%)
  between operations  15.4 us (2%)
    all_gather x1, waiting for transfers between devices, body(): lax.all_gather(regrouped, 'aux', axis=1, tiled=True)  433 us
    reduce_scatter x1, waiting for transfers between devices, body(): lax.psum_scatter(partial_value, 'rows', scatter_dimension=1, tiled=True)  235 us
    all_to_all x1, blocking collectives, body(): lax.all_to_all(b_rows, 'aux', split_axis=1, concat_axis=0, tiled=True)  77.9 us
    unnamed x1, blocking collectives  42 us
    dot_general x1, matrix products, contract(): lax.dot_general(left, right, (((0,), (0,)), ((), ())), preferred_element_...  34.5 us
  transfers between devices with their start and end apart: 2, of which 2 were waited for; matrix products, arithmetic and copies ran while one was open for 0% of the time, Pallas kernels for 0%

commit v1 on v0

--- a/solution.py
+++ b/solution.py
@@ -5,6 +5,28 @@
 
 NVIR = 1536
 NOCC_B = 4
+
+
+def laid_out(parts, dim):
+    shape = list(parts.shape[1:])
+    shape[dim] *= parts.shape[0]
+    return jnp.moveaxis(parts, 0, dim).reshape(shape)
+
+
+def collect(array, axis, dim):
+    peers = lax.axis_size(axis)
+    pairs = [(i, (i + 1) % peers) for i in range(peers)]
+    back = [(b, a) for a, b in pairs]
+    lower, upper = ([], [])
+    for step in range(peers - 1):
+        if step % 2 == 0:
+            lower.append(lax.ppermute(lower[-1] if lower else array, axis, pairs))
+        else:
+            upper.append(lax.ppermute(upper[-1] if upper else array, axis, back))
+    tiles = jnp.stack([*lower[::-1], array, *upper])
+    shift = lax.axis_index(axis) - len(lower)
+    tiles = tiles[(jnp.arange(peers) - shift) % peers]
+    return laid_out(tiles, dim)
 
 
 def row_weights(pairs, e_occ, e_vir, occ_batch, freq):
@@ -31,7 +53,7 @@
     regrouped = lax.all_to_all(b_rows, "aux", split_axis=1, concat_axis=0, tiled=True)
     weight = row_weights(group_pairs, e_occ, e_vir, occ_batch, freq)
     scaled = (weight[:, None] * regrouped.astype(jnp.float32)).astype(jnp.bfloat16)
-    partial_value = contract(scaled, lax.all_gather(regrouped, "aux", axis=1, tiled=True))
+    partial_value = contract(scaled, collect(regrouped, "aux", 1))
     return lax.psum_scatter(partial_value, "rows", scatter_dimension=1, tiled=True)
 
 

time: 843 us -> 942 us (1.12)
  waiting for transfers between devices: 668 us -> 556 us
  starting transfers between devices: 0.04 us -> 81.8 us
  local copies, waits for them, and re-layouts: 3.93 us -> 77.9 us
  blocking collectives: 120 us -> 148 us
  other arithmetic: 1.45 us -> 28.5 us
    all_gather x1 -> x0, waiting for transfers between devices: 433 us -> none  [body(): lax.all_gather(regrouped, 'aux', axis=1, tiled=True)]
    ppermute x0 -> x7, waiting for transfers between devices: none -> 321 us  [the longest x4 265 us: collect(): lower.append(lax.ppermute(lower[-1] if lower else array, axis, pairs))]
    ppermute x0 -> x7, starting transfers between devices: none -> 81.8 us  [the longest x3 75.3 us: collect(): upper.append(lax.ppermute(upper[-1] if upper else array, axis, back))]
    transpose x0 -> x1, local copies, waits for them, and re-layouts: none -> 32.8 us  [laid_out(): return jnp.moveaxis(parts, 0, dim).reshape(shape)]
    gather x0 -> x3, local copies, waits for them, and re-layouts: none -> 31 us  [collect(): tiles = tiles[(jnp.arange(peers) - shift) % peers]]
    unnamed x1, blocking collectives: 42 us -> 69.8 us
    transpose x0 -> x1, other arithmetic: none -> 24.8 us  [laid_out(): return jnp.moveaxis(parts, 0, dim).reshape(shape)]
    unnamed x9 -> x26, local copies, waits for them, and re-layouts: 0.82 us -> 10.6 us
  transfers between devices with their start and end apart: 2 -> 8, of which waited for: 2 -> 5; matrix products, arithmetic and copies ran while one was open for 0% -> 2% of each run, Pallas kernels for 0% -> 0%
where the time goes in v1:
time: 942 us; the launch traced here: 940 us
  waiting for transfers between devices  556 us (59%)
  blocking collectives  148 us (16%)
  starting transfers between devices  81.8 us (9%)
  local copies, waits for them, and re-layouts  77.9 us (8%)
  matrix products  32.9 us (3%)
  other arithmetic  28.5 us (3%)
  between operations  15.5 us (2%)
    ppermute x4, waiting for transfers between devices, collect(): lower.append(lax.ppermute(lower[-1] if lower else array, axis, pairs))  265 us
    reduce_scatter x1, waiting for transfers between devices, body(): lax.psum_scatter(partial_value, 'rows', scatter_dimension=1, tiled=True)  236 us
    all_to_all x1, blocking collectives, body(): lax.all_to_all(b_rows, 'aux', split_axis=1, concat_axis=0, tiled=True)  77.8 us
    ppermute x3, starting transfers between devices, collect(): upper.append(lax.ppermute(upper[-1] if upper else array, axis, back))  75.3 us
    unnamed x1, blocking collectives  69.8 us
    ppermute x3, waiting for transfers between devices, collect(): upper.append(lax.ppermute(upper[-1] if upper else array, axis, back))  55.5 us
    dot_general x1, matrix products, contract(): lax.dot_general(left, right, (((0,), (0,)), ((), ())), preferred_element_...  32.9 us
    transpose x1, local copies, waits for them, and re-layouts, laid_out(): return jnp.moveaxis(parts, 0, dim).reshape(shape)  32.8 us
  transfers between devices with their start and end apart: 8, of which 5 were waited for; matrix products, arithmetic and copies ran while one was open for 2% of the time, Pallas kernels for 0%

profile of v1, /device:TPU:0, one launch (start us, length us, event | category | flops | bytes accessed | tf_op | source)
XLA Modules:
  0.0 940.3 jit_solution(16573942885105325422)
XLA Ops:
  6.5 2.4 copy.19
  8.9 77.8 %all_to_all.19 = bf16[192,8,1024]{2,0,1:T(8,128)(2,1)S(1)} all-to-all(bf16[192,8,1024]{2,0,1:T(8,128)(2,1)S(1)} %bitcast.39), channel_id=1, replica_groups=mesh['rows'=4,'aux'=8] {'aux'}, dimensions={1} | all-to-all | bytes 6291456 | tf_op jit(solution)/shard_map/all_to_all | solution.py:53
  86.7 1.5 collective-permute-start
  88.2 69.9 %collective-permute-done = bf16[1536,1024]{1,0:T(8,128)(2,1)S(1)} collective-permute-done((bf16[1536,1024]{1,0:T(8,128)(2,1)S(1)}, bf16[1536,1024]{1,0:T(8,128)(2,1)S(1)}, u32[]{:S(2)}, u32[]{:S(2)}) %collective-permute-start) | collective-permute-done | bytes 3145760 | tf_op jit(solution)/shard_map/ppermute | solution.py:23
  158.1 4.7 collective-permute-start.4
  162.8 128.3 %collective-permute-done.1 = bf16[1536,1024]{1,0:T(8,128)(2,1)S(1)} collective-permute-done((bf16[1536,1024]{1,0:T(8,128)(2,1)S(1)}, bf16[1536,1024]{1,0:T(8,128)(2,1)S(1)}, u32[]{:S(2)}, u32[]{:S(2)}) %collective-permute-start.1) | collective-permute-done | bytes 3145760 | tf_op jit(solution)/shard_map/ppermute | solution.py:23
  291.1 2.5 collective-permute-start.2
  293.6 67.6 %collective-permute-start.5 = (bf16[1536,1024]{1,0:T(8,128)(2,1)}, bf16[1536,1024]{1,0:T(8,128)(2,1)}, u32[]{:S(2)}, u32[]{:S(2)}) collective-permute-start(bf16[1536,1024]{1,0:T(8,128)(2,1)} %collective-permute-done.4), channel_id=1, source_target_pairs={{1,0},{2,1},{3,2},{4,3},{5,4},{6,5},{7,6},{0,7},{9,8},{10,9},{11,1... | collective-permute-start | bytes 9437192 | tf_op jit(solution)/shard_map/ppermute | solution.py:25
  361.2 66.8 %collective-permute-done.2 = bf16[1536,1024]{1,0:T(8,128)(2,1)} collective-permute-done((bf16[1536,1024]{1,0:T(8,128)(2,1)S(1)}, bf16[1536,1024]{1,0:T(8,128)(2,1)}, u32[]{:S(2)}, u32[]{:S(2)}) %collective-permute-start.2) | collective-permute-done | bytes 3145760 | tf_op jit(solution)/shard_map/ppermute | solution.py:23
  428.1 2.6 collective-permute-start.3
  432.0 0.8 dynamic_slice.3
  432.7 0.6 dynamic-slice
  434.3 69.8 %all-reduce = s32[1536]{0:T(1024)S(1)} all-reduce(s32[1536]{0:T(1024)S(1)} %dynamic-update-slice), channel_id=1, replica_groups=mesh['rows'=4,'aux'=8] {'aux'}, use_global_device_ids=true, to_apply=%add | all-reduce | flops 1536 | bytes 12288
  504.2 1.3 select_reduce_fusion
  505.6 2.2 multiply_convert_fusion
  507.9 2.9 collective-permute-start.6
  510.8 2.2 bitcast_dynamic-update-slice_fusion.6
  513.0 2.2 bitcast_dynamic-update-slice_fusion.5
  515.2 0.3 bitcast_dynamic-update-slice_fusion.4
  515.5 0.3 bitcast_dynamic-update-slice_fusion.3
  515.9 0.3 constant_dynamic-update-slice_fusion
  516.2 2.2 bitcast_dynamic-update-slice_fusion.2
  518.4 2.2 bitcast_dynamic-update-slice_fusion.1
  520.6 55.5 %collective-permute-done.6 = bf16[1536,1024]{1,0:T(8,128)(2,1)S(1)} collective-permute-done((bf16[1536,1024]{1,0:T(8,128)(2,1)}, bf16[1536,1024]{1,0:T(8,128)(2,1)S(1)}, u32[]{:S(2)}, u32[]{:S(2)}) %collective-permute-start.6) | collective-permute-done | bytes 3145760 | tf_op jit(solution)/shard_map/ppermute | solution.py:25
  576.1 0.3 bitcast_dynamic-update-slice_fusion
  576.4 9.0 fusion.3
  585.4 11.0 %gather_fusion = bf16[8,768,1024]{2,1,0:T(8,128)(2,1)} fusion(bf16[8,768,1024]{2,1,0:T(8,128)(2,1)} %get-tuple-element.5, s32[1024]{0:T(1024)S(1)} %pad_clamp_fusion), kind=kCustom, calls=%fused_computation | custom fusion | bytes 25165856 | tf_op jit(solution)/shard_map/gather | solution.py:28
  596.4 10.9 %gather_fusion.1 = bf16[8,768,1024]{2,1,0:T(8,128)(2,1)} fusion(bf16[8,768,1024]{2,1,0:T(8,128)(2,1)} %get-tuple-element.6, s32[1024]{0:T(1024)S(1)} %pad_clamp_fusion), kind=kCustom, calls=%fused_computation.1 | custom fusion | bytes 25165856 | tf_op jit(solution)/shard_map/gather | solution.py:28
  607.3 24.8 %maximum_bitcast_fusion = bf16[1536,8,1024]{2,0,1:T(8,128)(2,1)} fusion(bf16[8,768,1024]{2,1,0:T(8,128)(2,1)} %gather_fusion.1, bf16[8,768,1024]{2,1,0:T(8,128)(2,1)} %gather_fusion), kind=kLoop, calls=%fused_computation.2 | loop fusion | flops 50331648 | bytes 50331648 | tf_op jit(solution)/shard_map/transpose | solution.py:13
  632.1 32.8 %copy.16 = bf16[1536,8,1024]{0,2,1:T(8,128)(2,1)} copy(bf16[1536,8,1024]{2,0,1:T(8,128)(2,1)} %maximum_bitcast_fusion) | data formatting | bytes 50331648 | tf_op jit(solution)/shard_map/transpose | solution.py:13
  665.0 32.9 %fusion.4 = f32[1024,8192]{1,0:T(8,128)} fusion(bf16[1536,1024]{1,0:T(8,128)(2,1)S(1)} %bitcast.41, bf16[1536,8192]{0,1:T(8,128)(2,1)} %bitcast.38), kind=kOutput, calls=%fused_computation.31 | convolution fusion | flops 25769803776 | bytes 61865984 | tf_op jit(solution)/shard_map/dot_general | solution.py:46
  697.9 235.6 %reduce-scatter.2.cloned.1.call-done = f32[1024,2048]{1,0:T(8,128)} async-done(((f32[1024,8192]{1,0:T(8,128)}), f32[1024,2048]{1,0:T(8,128)}) %reduce-scatter.2.cloned.1.call-update) | async-done | bytes 8388624 | tf_op jit(solution)/shard_map/reduce_scatter | solution.py:57
  (30 shorter events, 0.6 us)
Async XLA Ops:
  6.5 426.2 %copy-start.7 = (u32[32]{0:T(128)S(1)}, u32[32]{0:T(128)}, u32[]{:S(2)}) copy-start(u32[32]{0:T(128)} %constant.54) | copy-start | bytes 388
  6.5 427.4 %copy-start.5 = (s32[192]{0:T(256)S(1)}, s32[192]{0:T(256)}, u32[]{:S(2)}) copy-start(s32[192]{0:T(256)} %param.7) | copy-start | bytes 2308
  6.5 497.6 %copy-start.6 = (f32[1536]{0:T(1024)S(1)}, f32[1536]{0:T(1024)}, u32[]{:S(2)}) copy-start(f32[1536]{0:T(1024)} %param.9) | copy-start | bytes 18436
  6.5 926.9 %reduce-scatter.2.cloned.1.call-start = ((), (), s32[]{:S(2)}) async-start(), calls=%async_computation.2 | async-start | bytes 41943040 | tf_op jit(solution)/shard_map/reduce_scatter | solution.py:57
  86.7 71.4 %collective-permute-start = (bf16[1536,1024]{1,0:T(8,128)(2,1)S(1)}, bf16[1536,1024]{1,0:T(8,128)(2,1)S(1)}, u32[]{:S(2)}, u32[]{:S(2)}) collective-permute-start(bf16[1536,1024]{1,0:T(8,128)(2,1)S(1)} %bitcast.35), channel_id=1, source_target_pairs={{0,1},{1,2},{2,3},{3,4},{4,5},{5,6},{6,7},{7,0},{8,9},{9,10},{10,1... | collective-permute-start | bytes 9437192 | tf_op jit(solution)/shard_map/ppermute | solution.py:23
  158.1 135.5 %copy-start = (bf16[1536,1024]{1,0:T(8,128)(2,1)}, bf16[1536,1024]{1,0:T(8,128)(2,1)S(1)}, u32[]{:S(2)}) copy-start(bf16[1536,1024]{1,0:T(8,128)(2,1)S(1)} %collective-permute-done) | copy-start | bytes 9437188
  158.1 133.0 %collective-permute-start.1 = (bf16[1536,1024]{1,0:T(8,128)(2,1)S(1)}, bf16[1536,1024]{1,0:T(8,128)(2,1)S(1)}, u32[]{:S(2)}, u32[]{:S(2)}) collective-permute-start(bf16[1536,1024]{1,0:T(8,128)(2,1)S(1)} %collective-permute-done), channel_id=1, source_target_pairs={{0,1},{1,2},{2,3},{3,4},{4,5},{5,6},{6,7},{7,0},{8,9},{9,10},{10,1... | collective-permute-start | bytes 9437192 | tf_op jit(solution)/shard_map/ppermute | solution.py:23
  158.1 135.5 %collective-permute-start.4 = (bf16[1536,1024]{1,0:T(8,128)(2,1)S(1)}, bf16[1536,1024]{1,0:T(8,128)(2,1)}, u32[]{:S(2)}, u32[]{:S(2)}) collective-permute-start(bf16[1536,1024]{1,0:T(8,128)(2,1)S(1)} %bitcast.36), channel_id=1, source_target_pairs={{1,0},{2,1},{3,2},{4,3},{5,4},{6,5},{7,6},{0,7},{9,8},{10,9},{11,1... | collective-permute-start | bytes 9437192 | tf_op jit(solution)/shard_map/ppermute | solution.py:25
  291.1 70.1 %copy-start.2 = (bf16[1536,1024]{1,0:T(8,128)(2,1)}, bf16[1536,1024]{1,0:T(8,128)(2,1)S(1)}, u32[]{:S(2)}) copy-start(bf16[1536,1024]{1,0:T(8,128)(2,1)S(1)} %collective-permute-done.1) | copy-start | bytes 9437188
  291.1 137.0 %collective-permute-start.2 = (bf16[1536,1024]{1,0:T(8,128)(2,1)S(1)}, bf16[1536,1024]{1,0:T(8,128)(2,1)}, u32[]{:S(2)}, u32[]{:S(2)}) collective-permute-start(bf16[1536,1024]{1,0:T(8,128)(2,1)S(1)} %collective-permute-done.1), channel_id=1, source_target_pairs={{0,1},{1,2},{2,3},{3,4},{4,5},{5,6},{6,7},{7,0},{8,9},{9,10},{10,1... | collective-permute-start | bytes 9437192 | tf_op jit(solution)/shard_map/ppermute | solution.py:23
  293.6 214.3 %collective-permute-start.5 = (bf16[1536,1024]{1,0:T(8,128)(2,1)}, bf16[1536,1024]{1,0:T(8,128)(2,1)}, u32[]{:S(2)}, u32[]{:S(2)}) collective-permute-start(bf16[1536,1024]{1,0:T(8,128)(2,1)} %collective-permute-done.4), channel_id=1, source_target_pairs={{1,0},{2,1},{3,2},{4,3},{5,4},{6,5},{7,6},{0,7},{9,8},{10,9},{11,1... | collective-permute-start | bytes 9437192 | tf_op jit(solution)/shard_map/ppermute | solution.py:25
  428.1 82.7 %collective-permute-start.3 = (bf16[1536,1024]{1,0:T(8,128)(2,1)}, bf16[1536,1024]{1,0:T(8,128)(2,1)}, u32[]{:S(2)}, u32[]{:S(2)}) collective-permute-start(bf16[1536,1024]{1,0:T(8,128)(2,1)} %collective-permute-done.2), channel_id=1, source_target_pairs={{0,1},{1,2},{2,3},{3,4},{4,5},{5,6},{6,7},{7,0},{8,9},{9,10},{10,1... | collective-permute-start | bytes 9437192 | tf_op jit(solution)/shard_map/ppermute | solution.py:23
  505.6 9.6 %copy-start.3 = (bf16[1536,1024]{1,0:T(8,128)(2,1)S(1)}, bf16[1536,1024]{1,0:T(8,128)(2,1)}, u32[]{:S(2)}) copy-start(bf16[1536,1024]{1,0:T(8,128)(2,1)} %copy-done.2) | copy-start | bytes 9437188
  505.6 9.9 %copy-start.1 = (bf16[1536,1024]{1,0:T(8,128)(2,1)S(1)}, bf16[1536,1024]{1,0:T(8,128)(2,1)}, u32[]{:S(2)}) copy-start(bf16[1536,1024]{1,0:T(8,128)(2,1)} %copy-done) | copy-start | bytes 9437188
  507.9 68.2 %collective-permute-start.6 = (bf16[1536,1024]{1,0:T(8,128)(2,1)}, bf16[1536,1024]{1,0:T(8,128)(2,1)S(1)}, u32[]{:S(2)}, u32[]{:S(2)}) collective-permute-start(bf16[1536,1024]{1,0:T(8,128)(2,1)} %collective-permute-done.5), channel_id=1, source_target_pairs={{1,0},{2,1},{3,2},{4,3},{5,4},{6,5},{7,6},{0,7},{9,8},{10,9},{11,1... | collective-permute-start | bytes 9437192 | tf_op jit(solution)/shard_map/ppermute | solution.py:25
  632.1 32.8 %copy-start.4 = (bf16[8,192,1024]{2,1,0:T(8,128)(2,1)S(1)}, bf16[8,192,1024]{2,1,0:T(8,128)(2,1)}, u32[]{:S(2)}) copy-start(bf16[8,192,1024]{2,1,0:T(8,128)(2,1)} %multiply_convert_fusion) | copy-start | bytes 9437188
Sparse Core Ops, SparseCore 0:
  698.0 235.4 reduce-scatter.1
